TPU v7x, 512 devices: a whole 4x8x8 slice. The times are simulated.
512 devices in a mesh: seq: 64 (over z_hi, y, core), ch: 8 (over x, z_lo).
Axes of the slice: x: 4, y: 8, z: 8 (z_hi: 4, z_lo: 2; z = z_hi * 2 + z_lo), core: 2. Of those that a mesh axis runs over, the one named last changes fastest.
Arguments:
- inputs: bfloat16 [262144, 2048], P('seq', 'ch'), may hold values from -6 to 6
- first_factor: bfloat16 [512, 512], P('ch'), may hold values from -0.25 to 0.25
- twiddle: float32 [512, 512], P('seq'), may hold values from -4 to 4
- second_factor: bfloat16 [512, 512], P('ch'), may hold values from -0.25 to 0.25
- block_first: bfloat16 [64, 32, 32], P('ch'), may hold values from -1 to 1
- block_second: bfloat16 [32, 64, 64], P('ch'), may hold values from -0.75 to 0.75
Outputs:
- mixed_out: bfloat16 [262144, 2048], P('seq', 'ch')
All inputs are finite; a program needn't handle non-finite values.
Results may differ from a plain program's by a relative error of at most 0.007.
Values may be sent and summed in bfloat16 or wider, within the bound.
No kernel may reach another device: no remote copies, remote signals or barrier semaphores. Data moves between devices by JAX's collectives and lax.ppermute only.
A program may use at most 128 MiB of HBM per device.

v0:
```python
import jax
import jax.numpy as jnp
from jax import lax
from jax.sharding import PartitionSpec as P

BLOCK = 512
CHUNKS = 1


def channel_weights(block_first, block_second, n_ch):
    n_a, n_m, n_b = block_first.shape
    m_l = n_m // n_ch
    bf = jnp.transpose(block_first, (1, 0, 2))
    bf = bf.reshape(n_ch, m_l, n_a, 1, n_b)
    eye_a = jnp.eye(n_a, dtype=jnp.bool_).reshape(1, 1, n_a, n_a, 1)
    w1t = jnp.where(eye_a, bf, jnp.zeros((), bf.dtype))
    w1t = w1t.reshape(n_ch * m_l * n_a, n_a * n_b)
    n_m2, n_p, n_a2 = block_second.shape
    a_l = n_a2 // n_ch
    bs = block_second.reshape(n_m2, n_p, n_ch, a_l)
    bs = jnp.transpose(bs, (2, 0, 3, 1))
    bs = bs.reshape(n_ch, n_m2, a_l, 1, n_p)
    eye_m = jnp.eye(n_m2, dtype=jnp.bool_).reshape(1, n_m2, 1, n_m2, 1)
    w2 = jnp.where(eye_m, bs, jnp.zeros((), bs.dtype))
    w2 = w2.reshape(n_ch * n_m2 * a_l, n_m2 * n_p)
    return (w1t, w2)


def make_local(n_seq, n_ch):

    def local(inputs, first_factor, twiddle, second_factor, block_first, block_second):
        tok_rows, channels = inputs.shape
        outer_rows = tok_rows // BLOCK
        token_grid = inputs.reshape(outer_rows, BLOCK, channels)
        rows = first_factor.shape[0]
        pair = jnp.concatenate([first_factor, second_factor], axis=0)
        spread = jnp.broadcast_to(pair[None], (n_ch,) + pair.shape)
        both = lax.all_to_all(spread, "ch", split_axis=0, concat_axis=0, tiled=True)
        both = both.reshape(n_ch, 2, rows, BLOCK)
        full_first = both[:, 0].reshape(BLOCK, BLOCK)
        full_second = both[:, 1].reshape(BLOCK, BLOCK)
        twiddle_t = jnp.transpose(twiddle)
        token_f32 = lax.optimization_barrier(token_grid)
        w1t, w2 = channel_weights(block_first, block_second, n_ch)
        contract = (((1,), (1,)), ((), ()))
        width = BLOCK // CHUNKS
        outs = []
        for q in range(CHUNKS):
            lo = q * width
            first = lax.dot_general(
                full_first[lo : lo + width],
                token_grid,
                contract,
                preferred_element_type=jnp.float32,
            )
            twisted = (first * twiddle_t[lo : lo + width, :, None]).astype(jnp.bfloat16)
            twisted, w1t, w2 = lax.optimization_barrier((twisted, w1t, w2))
            gathered = lax.all_to_all(twisted, "seq", split_axis=0, concat_axis=1, tiled=True)
            mixed = lax.dot_general(
                full_second, gathered, contract, preferred_element_type=jnp.float32
            ).astype(jnp.bfloat16)
            returned = lax.all_to_all(mixed, "seq", split_axis=0, concat_axis=1, tiled=True)
            gated = (
                token_f32[:, lo : lo + width].astype(jnp.float32) * returned.astype(jnp.float32)
            ).astype(jnp.bfloat16)
            gated = gated.reshape(outer_rows * width, channels)
            middle_t = lax.dot_general(
                w1t, gated, contract, preferred_element_type=jnp.float32
            ).astype(jnp.bfloat16)
            middle_t = middle_t.reshape(n_ch, channels // n_ch, outer_rows * width)
            recv = lax.all_to_all(middle_t, "ch", split_axis=0, concat_axis=0, tiled=True)
            recv = recv.reshape(channels, outer_rows * width)
            result = lax.dot_general(
                recv, w2, (((0,), (0,)), ((), ())), preferred_element_type=jnp.float32
            ).astype(jnp.bfloat16)
            outs.append(result.reshape(outer_rows, width, channels))
        out = jnp.concatenate(outs, axis=1)
        return out.reshape(tok_rows, channels)

    return local


def solution(mesh):
    placed = (
        P("seq", "ch"),
        P("ch", None),
        P("seq", None),
        P("ch", None),
        P("ch", None, None),
        P("ch", None, None),
    )
    return jax.shard_map(
        make_local(mesh.shape["seq"], mesh.shape["ch"]),
        mesh=mesh,
        in_specs=placed,
        out_specs=P("seq", "ch"),
        check_vma=False,
    )
```

profile of v0, /device:TPU:41, one launch (start us, length us, event | category | flops | bytes accessed | tf_op | source)
XLA Modules:
  0.0 202.5 jit_solution(12817067652406120706)
XLA Ops:
  0.0 0.0 copy-start.1
  0.0 0.0 copy-start.2
  0.0 0.9 pad_maximum_fusion
  0.9 1.1 broadcast_in_dim.49
  2.0 5.8 %all-to-all-start = ((bf16[8,128,512]{2,1,0:T(8,128)(2,1)}), bf16[8,128,512]{2,1,0:T(8,128)(2,1)S(1)}, u32[]{:S(2)}, u32[]{:S(2)}) async-start(bf16[8,128,512]{2,1,0:T(8,128)(2,1)} %broadcast_in_dim.49), calls=%async_computation | async-start | bytes 2097152 | tf_op jit(solution)/shard_map/all_to_all | solution.py:38
  7.8 0.0 copy-done.1
  7.8 0.6 copy.16
  8.5 0.0 copy-done.2
  8.5 0.0 copy-start
  8.5 0.0 copy-start.3
  8.5 0.1 copy.17
  8.6 0.2 broadcast_select_fusion.1
  8.8 0.2 select_n.19
  9.0 1.8 broadcast_select_fusion
  10.9 1.4 select_n.17
  12.3 10.1 %all-to-all-done = bf16[8,128,512]{2,1,0:T(8,128)(2,1)S(1)} async-done(((bf16[8,128,512]{2,1,0:T(8,128)(2,1)}), bf16[8,128,512]{2,1,0:T(8,128)(2,1)S(1)}, u32[]{:S(2)}, u32[]{:S(2)}) %all-to-all-start) | async-done | bytes 1048608 | tf_op jit(solution)/shard_map/all_to_all | solution.py:38
  22.4 0.1 fusion.7
  22.5 0.0 copy-done
  22.5 0.0 copy-done.3
  22.5 1.5 multiply_convert_fusion
  24.0 1.2 copy.19
  25.2 74.3 %all_to_all.37 = bf16[512,8,256]{2,1,0:T(8,128)(2,1)S(1)} all-to-all(bf16[512,8,256]{2,1,0:T(8,128)(2,1)S(1)} %copy.19), channel_id=1, replica_groups=mesh['seq'=64,'ch'=8] {'seq'}, dimensions={0} | all-to-all | bytes 4194304 | tf_op jit(solution)/shard_map/all_to_all | solution.py:58
  99.5 1.3 fusion.4
  100.7 2.5 %copy.21 = bf16[512,8,256]{2,1,0:T(8,128)(2,1)} copy(bf16[512,8,256]{2,0,1:T(8,128)(2,1)S(1)} %fusion.4) | data formatting | bytes 4194304 | tf_op jit(solution)/shard_map/convert_element_type | solution.py:61
  103.2 8.7 %all-to-all-start.2 = ((bf16[512,8,256]{2,1,0:T(8,128)(2,1)}), bf16[512,8,256]{2,1,0:T(8,128)(2,1)S(1)}, u32[]{:S(2)}, u32[]{:S(2)}) async-start(bf16[512,8,256]{2,1,0:T(8,128)(2,1)} %copy.21), calls=%async_computation.2 | async-start | bytes 4194304 | tf_op jit(solution)/shard_map/all_to_all | solution.py:62
  111.9 52.2 %all-to-all-done.2 = bf16[512,8,256]{2,1,0:T(8,128)(2,1)S(1)} async-done(((bf16[512,8,256]{2,1,0:T(8,128)(2,1)}), bf16[512,8,256]{2,1,0:T(8,128)(2,1)S(1)}, u32[]{:S(2)}, u32[]{:S(2)}) %all-to-all-start.2) | async-done | bytes 2097184 | tf_op jit(solution)/shard_map/all_to_all | solution.py:62
  164.1 2.1 %fusion = bf16[8,512,256]{2,1,0:T(8,128)(2,1)S(1)} fusion(bf16[8,512,256]{2,1,0:T(8,128)(2,1)} %bitcast.52, bf16[64,8,8,256]{3,2,1,0:T(8,128)(2,1)S(1)} %bitcast.48), kind=kLoop, calls=%fused_computation.4 | loop fusion | flops 4194304 | bytes 6291456 | tf_op jit(solution)/shard_map/convert_element_type | solution.py:65
  166.2 0.7 convolution_convert_fusion.1
  166.9 33.5 %all_to_all.38 = bf16[8,32,4096]{2,1,0:T(8,128)(2,1)S(1)} all-to-all(bf16[8,32,4096]{2,1,0:T(8,128)(2,1)S(1)} %bitcast.50), channel_id=1, replica_groups=mesh['seq'=64,'ch'=8] {'ch'}, dimensions={0} | all-to-all | bytes 4194304 | tf_op jit(solution)/shard_map/all_to_all | solution.py:71
  200.5 2.1 %convolution_convert_fusion = bf16[4096,256]{1,0:T(8,128)(2,1)} fusion(bf16[256,4096]{1,0:T(8,128)(2,1)S(1)} %bitcast.47, bf16[256,256]{1,0:T(8,128)(2,1)S(1)} %select_n.19), kind=kOutput, calls=%fused_computation | convolution fusion | flops 537919488 | bytes 4325376 | tf_op jit(solution)/shard_map/dot_general | solution.py:73
  (2 shorter events, 0.0 us)
Async XLA Ops:
  0.0 7.8 %copy-start.1 = (bf16[8,32,32]{2,1,0:T(8,128)(2,1)S(1)}, bf16[8,32,32]{2,1,0:T(8,128)(2,1)}, u32[]{:S(2)}) copy-start(bf16[8,32,32]{2,1,0:T(8,128)(2,1)} %param.10) | copy-start | bytes 49156
  0.0 8.5 %copy-start.2 = (bf16[4,64,64]{2,1,0:T(8,128)(2,1)S(1)}, bf16[4,64,64]{2,1,0:T(8,128)(2,1)}, u32[]{:S(2)}) copy-start(bf16[4,64,64]{2,1,0:T(8,128)(2,1)} %param.11) | copy-start | bytes 98308
  2.0 20.4 %all-to-all-start = ((bf16[8,128,512]{2,1,0:T(8,128)(2,1)}), bf16[8,128,512]{2,1,0:T(8,128)(2,1)S(1)}, u32[]{:S(2)}, u32[]{:S(2)}) async-start(bf16[8,128,512]{2,1,0:T(8,128)(2,1)} %broadcast_in_dim.49), calls=%async_computation | async-start | bytes 2097152 | tf_op jit(solution)/shard_map/all_to_all | solution.py:38
  8.5 14.0 %copy-start = (bf16[4096,256]{1,0:T(8,128)(2,1)S(1)}, bf16[4096,256]{1,0:T(8,128)(2,1)}, u32[]{:S(2)}) copy-start(bf16[4096,256]{1,0:T(8,128)(2,1)} %param.6) | copy-start | bytes 6291460
  8.5 14.0 %copy-start.3 = (f32[8,512]{1,0:T(8,128)S(1)}, f32[8,512]{1,0:T(8,128)}, u32[]{:S(2)}) copy-start(f32[8,512]{1,0:T(8,128)} %param.8) | copy-start | bytes 49156
  103.2 60.8 %all-to-all-start.2 = ((bf16[512,8,256]{2,1,0:T(8,128)(2,1)}), bf16[512,8,256]{2,1,0:T(8,128)(2,1)S(1)}, u32[]{:S(2)}, u32[]{:S(2)}) async-start(bf16[512,8,256]{2,1,0:T(8,128)(2,1)} %copy.21), calls=%async_computation.2 | async-start | bytes 4194304 | tf_op jit(solution)/shard_map/all_to_all | solution.py:62
where the time goes:
time: 203 us
  blocking collectives  108 us (53%)
  waiting for transfers between devices  62.2 us (31%)
  starting transfers between devices  14.5 us (7%)
  local copies, waits for them, and re-layouts  7.24 us (4%)
  matrix products  5.56 us (3%)
  other arithmetic  5.05 us (2%)
    all_to_all x1, blocking collectives, local(): lax.all_to_all(twisted, 'seq', split_axis=0, concat_axis=1, tiled=True)  74.3 us
    all_to_all x1, waiting for transfers between devices, local(): lax.all_to_all(mixed, 'seq', split_axis=0, concat_axis=1, tiled=True)  52.2 us
    all_to_all x1, blocking collectives, local(): lax.all_to_all(middle_t, 'ch', split_axis=0, concat_axis=0, tiled=True)  33.5 us
    all_to_all x1, waiting for transfers between devices, local(): both = lax.all_to_all(spread, 'ch', split_axis=0, concat_axis=0, tiled=True)  10.1 us
    all_to_all x1, starting transfers between devices, local(): lax.all_to_all(mixed, 'seq', split_axis=0, concat_axis=1, tiled=True)  8.66 us
    all_to_all x1, starting transfers between devices, local(): both = lax.all_to_all(spread, 'ch', split_axis=0, concat_axis=0, tiled=True)  5.83 us
  transfers between devices with their start and end apart: 2, of which 2 were waited for; matrix products, arithmetic and copies ran while one was open for 2% of the time, Pallas kernels for 0%

commit v1 on v0

--- a/solution.py
+++ b/solution.py
@@ -5,6 +5,13 @@
 
 BLOCK = 512
 CHUNKS = 1
+
+
+def trade_parts(x, axis, split, join):
+    devices = lax.axis_size(axis)
+    blocks = jnp.stack(jnp.split(x, devices, axis=split), axis=0)
+    blocks = lax.all_to_all(blocks, axis, split_axis=0, concat_axis=0)
+    return jnp.concatenate(blocks, axis=join)
 
 
 def channel_weights(block_first, block_second, n_ch):
@@ -59,7 +66,7 @@
             mixed = lax.dot_general(
                 full_second, gathered, contract, preferred_element_type=jnp.float32
             ).astype(jnp.bfloat16)
-            returned = lax.all_to_all(mixed, "seq", split_axis=0, concat_axis=1, tiled=True)
+            returned = trade_parts(mixed, "seq", 0, 1)
             gated = (
                 token_f32[:, lo : lo + width].astype(jnp.float32) * returned.astype(jnp.float32)
             ).astype(jnp.bfloat16)

time: 203 us -> 241 us (1.19)
  local copies, waits for them, and re-layouts: 7.24 us -> 43.7 us
  waiting for transfers between devices: 62.2 us -> 65.6 us
    unnamed x9 -> x74, local copies, waits for them, and re-layouts: 0.12 us -> 40.1 us
    all_to_all x1, waiting for transfers between devices: 10.1 us -> 13.5 us  [local(): both = lax.all_to_all(spread, 'ch', split_axis=0, concat_axis=0, tiled=True)]
    convert_element_type x1 -> x0, local copies, waits for them, and re-layouts: 2.5 us -> none  [local(): mixed = lax.dot_general(full_second, gathered, contract, preferred_elemen...]
  transfers between devices with their start and end apart: 2 -> 2, of which waited for: 2 -> 2; matrix products, arithmetic and copies ran while one was open for 2% -> 0% of each run, Pallas kernels for 0% -> 0%
where the time goes in v1:
time: 241 us
  blocking collectives  108 us (45%)
  waiting for transfers between devices  65.6 us (27%)
  local copies, waits for them, and re-layouts  43.7 us (18%)
  starting transfers between devices  14.5 us (6%)
  matrix products  5.57 us (2%)
  other arithmetic  3.38 us (1%)
    all_to_all x1, blocking collectives, local(): lax.all_to_all(twisted, 'seq', split_axis=0, concat_axis=1, tiled=True)  74.3 us
    all_to_all x1, waiting for transfers between devices, trade_parts(): blocks = lax.all_to_all(blocks, axis, split_axis=0, concat_axis=0)  52.2 us
    unnamed x74, local copies, waits for them, and re-layouts  40.1 us
    all_to_all x1, blocking collectives, local(): lax.all_to_all(middle_t, 'ch', split_axis=0, concat_axis=0, tiled=True)  33.5 us
    all_to_all x1, waiting for transfers between devices, local(): both = lax.all_to_all(spread, 'ch', split_axis=0, concat_axis=0, tiled=True)  13.5 us
    all_to_all x1, starting transfers between devices, trade_parts(): blocks = lax.all_to_all(blocks, axis, split_axis=0, concat_axis=0)  8.66 us
    all_to_all x1, starting transfers between devices, local(): both = lax.all_to_all(spread, 'ch', split_axis=0, concat_axis=0, tiled=True)  5.83 us
  transfers between devices with their start and end apart: 2, of which 2 were waited for; matrix products, arithmetic and copies ran while one was open for 0% of the time, Pallas kernels for 0%

profile of v1, /device:TPU:41, one launch (start us, length us, event | category | flops | bytes accessed | tf_op | source)
XLA Modules:
  0.0 240.8 jit_solution(4558365037833800233)
XLA Ops:
  0.0 0.9 pad_maximum_fusion
  0.9 1.1 broadcast_in_dim.49
  2.0 5.8 %all-to-all-start = ((bf16[8,128,512]{2,1,0:T(8,128)(2,1)}), bf16[8,128,512]{2,1,0:T(8,128)(2,1)S(1)}, u32[]{:S(2)}, u32[]{:S(2)}) async-start(bf16[8,128,512]{2,1,0:T(8,128)(2,1)} %broadcast_in_dim.49), calls=%async_computation | async-start | bytes 2097152 | tf_op jit(solution)/shard_map/all_to_all | solution.py:45
  8.9 13.5 %all-to-all-done = bf16[8,128,512]{2,1,0:T(8,128)(2,1)S(1)} async-done(((bf16[8,128,512]{2,1,0:T(8,128)(2,1)}), bf16[8,128,512]{2,1,0:T(8,128)(2,1)S(1)}, u32[]{:S(2)}, u32[]{:S(2)}) %all-to-all-start) | async-done | bytes 1048608 | tf_op jit(solution)/shard_map/all_to_all | solution.py:45
  22.5 1.5 multiply_convert_fusion
  24.0 1.2 copy.19
  25.2 74.3 %all_to_all.33 = bf16[512,8,256]{2,1,0:T(8,128)(2,1)S(1)} all-to-all(bf16[512,8,256]{2,1,0:T(8,128)(2,1)S(1)} %copy.19), channel_id=1, replica_groups=mesh['seq'=64,'ch'=8] {'seq'}, dimensions={0} | all-to-all | bytes 4194304 | tf_op jit(solution)/shard_map/all_to_all | solution.py:65
  99.5 1.3 fusion.4
  100.7 0.6 constant_dynamic-update-slice_fusion.63
  101.4 0.6 constant_dynamic-update-slice_fusion.62
  102.0 0.6 constant_dynamic-update-slice_fusion.61
  102.6 0.6 constant_dynamic-update-slice_fusion.60
  103.2 0.6 constant_dynamic-update-slice_fusion.59
  103.8 0.6 constant_dynamic-update-slice_fusion.58
  104.4 0.6 constant_dynamic-update-slice_fusion.57
  105.1 0.6 constant_dynamic-update-slice_fusion.56
  105.7 0.6 constant_dynamic-update-slice_fusion.55
  106.3 0.6 constant_dynamic-update-slice_fusion.54
  106.9 0.6 constant_dynamic-update-slice_fusion.53
  107.5 0.6 constant_dynamic-update-slice_fusion.52
  108.2 0.6 constant_dynamic-update-slice_fusion.51
  108.8 0.6 constant_dynamic-update-slice_fusion.50
  109.4 0.6 constant_dynamic-update-slice_fusion.49
  110.0 0.6 constant_dynamic-update-slice_fusion.48
  110.6 0.6 constant_dynamic-update-slice_fusion.47
  111.3 0.6 constant_dynamic-update-slice_fusion.46
  111.9 0.6 constant_dynamic-update-slice_fusion.45
  112.5 0.6 constant_dynamic-update-slice_fusion.44
  113.1 0.6 constant_dynamic-update-slice_fusion.43
  113.7 0.6 constant_dynamic-update-slice_fusion.42
  114.4 0.6 constant_dynamic-update-slice_fusion.41
  115.0 0.6 constant_dynamic-update-slice_fusion.40
  115.6 0.6 constant_dynamic-update-slice_fusion.39
  116.2 0.6 constant_dynamic-update-slice_fusion.38
  116.8 0.6 constant_dynamic-update-slice_fusion.37
  117.5 0.6 constant_dynamic-update-slice_fusion.36
  118.1 0.6 constant_dynamic-update-slice_fusion.35
  118.7 0.6 constant_dynamic-update-slice_fusion.34
  119.3 0.6 constant_dynamic-update-slice_fusion.33
  119.9 0.6 constant_dynamic-update-slice_fusion.32
  120.6 0.6 constant_dynamic-update-slice_fusion.31
  121.2 0.6 constant_dynamic-update-slice_fusion.30
  121.8 0.6 constant_dynamic-update-slice_fusion.29
  122.4 0.6 constant_dynamic-update-slice_fusion.28
  123.0 0.6 constant_dynamic-update-slice_fusion.27
  123.7 0.6 constant_dynamic-update-slice_fusion.26
  124.3 0.6 constant_dynamic-update-slice_fusion.25
  124.9 0.6 constant_dynamic-update-slice_fusion.24
  125.5 0.6 constant_dynamic-update-slice_fusion.23
  127.4 0.6 constant_dynamic-update-slice_fusion.20
  129.2 0.6 constant_dynamic-update-slice_fusion.17
  131.1 0.6 constant_dynamic-update-slice_fusion.14
  132.9 0.6 constant_dynamic-update-slice_fusion.11
  134.8 0.6 constant_dynamic-update-slice_fusion.8
  135.4 0.6 constant_dynamic-update-slice_fusion.7
  137.3 0.6 constant_dynamic-update-slice_fusion.4
  139.1 0.6 constant_dynamic-update-slice_fusion.1
  140.4 8.7 %all-to-all-start.2 = ((bf16[64,8,8,256]{3,1,2,0:T(8,128)(2,1)}), bf16[64,8,8,256]{3,1,2,0:T(8,128)(2,1)S(1)}, u32[]{:S(2)}, u32[]{:S(2)}) async-start(bf16[64,8,8,256]{3,1,2,0:T(8,128)(2,1)} %constant_dynamic-update-slice_fusion), calls=%async_computation.2 | async-start | bytes 4194304 | tf_op jit(solution)/shard_map/all_to_all | solution.py:13
  149.0 52.2 %all-to-all-done.2 = bf16[64,8,8,256]{3,1,2,0:T(8,128)(2,1)S(1)} async-done(((bf16[64,8,8,256]{3,1,2,0:T(8,128)(2,1)}), bf16[64,8,8,256]{3,1,2,0:T(8,128)(2,1)S(1)}, u32[]{:S(2)}, u32[]{:S(2)}) %all-to-all-start.2) | async-done | bytes 2097184 | tf_op jit(solution)/shard_map/all_to_all | solution.py:13
  201.8 1.0 copy-done.1
  202.8 1.6 fusion
  204.4 0.7 convolution_convert_fusion.1
  205.2 33.5 %all_to_all.34 = bf16[8,32,4096]{2,1,0:T(8,128)(2,1)S(1)} all-to-all(bf16[8,32,4096]{2,1,0:T(8,128)(2,1)S(1)} %bitcast.299), channel_id=1, replica_groups=mesh['seq'=64,'ch'=8] {'ch'}, dimensions={0} | all-to-all | bytes 4194304 | tf_op jit(solution)/shard_map/all_to_all | solution.py:78
  238.7 2.1 convolution_convert_fusion
  (34 shorter events, 11.0 us)
Async XLA Ops:
  0.0 7.8 %copy-start.2 = (bf16[8,32,32]{2,1,0:T(8,128)(2,1)S(1)}, bf16[8,32,32]{2,1,0:T(8,128)(2,1)}, u32[]{:S(2)}) copy-start(bf16[8,32,32]{2,1,0:T(8,128)(2,1)} %param.10) | copy-start | bytes 49156
  0.0 7.9 %copy-start.3 = (bf16[4,64,64]{2,1,0:T(8,128)(2,1)S(1)}, bf16[4,64,64]{2,1,0:T(8,128)(2,1)}, u32[]{:S(2)}) copy-start(bf16[4,64,64]{2,1,0:T(8,128)(2,1)} %param.11) | copy-start | bytes 98308
  2.0 20.4 %all-to-all-start = ((bf16[8,128,512]{2,1,0:T(8,128)(2,1)}), bf16[8,128,512]{2,1,0:T(8,128)(2,1)S(1)}, u32[]{:S(2)}, u32[]{:S(2)}) async-start(bf16[8,128,512]{2,1,0:T(8,128)(2,1)} %broadcast_in_dim.49), calls=%async_computation | async-start | bytes 2097152 | tf_op jit(solution)/shard_map/all_to_all | solution.py:45
  7.9 14.6 %copy-start.4 = (f32[8,512]{1,0:T(8,128)S(1)}, f32[8,512]{1,0:T(8,128)}, u32[]{:S(2)}) copy-start(f32[8,512]{1,0:T(8,128)} %param.8) | copy-start | bytes 49156
  8.9 13.6 %copy-start = (bf16[4096,256]{1,0:T(8,128)(2,1)S(1)}, bf16[4096,256]{1,0:T(8,128)(2,1)}, u32[]{:S(2)}) copy-start(bf16[4096,256]{1,0:T(8,128)(2,1)} %param.6) | copy-start | bytes 6291460
  140.4 60.9 %all-to-all-start.2 = ((bf16[64,8,8,256]{3,1,2,0:T(8,128)(2,1)}), bf16[64,8,8,256]{3,1,2,0:T(8,128)(2,1)S(1)}, u32[]{:S(2)}, u32[]{:S(2)}) async-start(bf16[64,8,8,256]{3,1,2,0:T(8,128)(2,1)} %constant_dynamic-update-slice_fusion), calls=%async_computation.2 | async-start | bytes 4194304 | tf_op jit(solution)/shard_map/all_to_all | solution.py:13
  201.2 1.6 copy-start.1
